TPU v7x, 256 devices: a whole 4x4x8 slice. The times are simulated.
256 devices in a mesh: pipe: 2 (over core), seq: 4 (over x), tensor: 32 (over z, y).
Axes of the slice: x: 4, y: 4, z: 8, core: 2. Of those that a mesh axis runs over, the one named last changes fastest.
Arguments:
- token_ids: int32 [2, 768], P(None, 'seq'), may hold values from 0 to 511
- embed_table: bfloat16 [512, 8192], P(None, 'tensor'), may hold values from -24 to 24
- in_proj: bfloat16 [2, 8192, 3, 4096], P('pipe', None, None, 'tensor'), may hold values from -0.0625 to 0.0625
- feat_taps: float32 [2, 3, 3, 4096], P('pipe', None, None, 'tensor'), may hold values from -3 to 3
- se_taps: float32 [7, 4096], P(None, 'tensor'), may hold values from -2 to 2
- mr_taps: float32 [128, 4096], P(None, 'tensor'), may hold values from -0.6 to 0.6
- out_proj: bfloat16 [2, 4096, 8192], P('pipe', 'tensor'), may hold values from -0.1875 to 0.1875
- norm_gain: bfloat16 [2, 8192], P('pipe', 'tensor'), may hold values from 0.25 to 1.75
Outputs:
- segment_out: bfloat16 [2, 2, 768, 8192], P('pipe', None, 'seq', 'tensor')
All inputs are finite; a program needn't handle non-finite values.
Results may differ from a plain program's by a relative error of at most 0.023.
Values may be sent and summed in bfloat16 or wider, within the bound.
No kernel may reach another device: no remote copies, remote signals or barrier semaphores. Data moves between devices by JAX's collectives and lax.ppermute only.
A program may use at most 64 MiB of HBM per device.

v0:
```python
import jax
import jax.numpy as jnp
from jax import lax
from jax.sharding import PartitionSpec as P

VOCAB = 512
KL = 128
KS = 7
KF = 3
SEGMENTS = 2
HALO = 129


epsilon = 1e-06


def from_behind(value, axis, steps):
    count = lax.axis_size(axis)
    pairs = [(source, (source + steps) % count) for source in range(count)]
    return lax.ppermute(value, axis, pairs)


def passed_along(value, axis, steps):
    count = lax.axis_size(axis)
    first, last = (max(0, -steps), min(count, count - steps))
    return lax.ppermute(value, axis, [(source, source + steps) for source in range(first, last)])


def project(stream, w_flat, gain_cols):
    gathered, gain_all = (
        lax.all_gather(stream, "tensor", axis=2, tiled=True),
        lax.all_gather(gain_cols, "tensor", axis=1, tiled=True),
    )
    values = gathered.astype(jnp.float32)
    inv_rms = lax.rsqrt(jnp.mean(values * values, axis=2, keepdims=True) + epsilon)
    normed = (values * inv_rms * gain_all[0].astype(jnp.float32)).astype(jnp.bfloat16)
    projected = jnp.einsum("snd,dk->snk", normed, w_flat, preferred_element_type=jnp.float32)
    return projected.astype(jnp.bfloat16)


def send_tails(projected):
    row_count = projected.shape[1]
    chan_local = projected.shape[2] // 3
    kv_tail = projected[:, row_count - HALO :, chan_local:]
    q_tail = projected[:, row_count - (KF - 1) :, :chan_local]
    return from_behind((kv_tail, q_tail), "seq", 1)


def hand_over(result):
    return passed_along(result, "pipe", 1)


def mixing(stream, projected, kv_prev, q_prev, feat_local, long_taps, w_down):
    row_count = projected.shape[1]
    chan_local = projected.shape[2] // 3
    q_all = jnp.concatenate([q_prev, projected[:, :, :chan_local]], axis=1).astype(jnp.float32)
    kv_all = jnp.concatenate([kv_prev, projected[:, :, chan_local:]], axis=1).astype(jnp.float32)
    q_taps = feat_local[0, :, 0, :]
    kv_taps = feat_local[0, :, 1:, :].reshape(KF, 2 * chan_local)
    kv_span = KL - 1 + row_count
    q_feat = jnp.zeros((projected.shape[0], row_count, chan_local), jnp.float32)
    kv_feat = jnp.zeros((projected.shape[0], kv_span, 2 * chan_local), jnp.float32)
    for tap_index in range(KF):
        offset = KF - 1 - tap_index
        q_feat = q_feat + q_taps[tap_index] * q_all[:, offset : offset + row_count]
        kv_feat = kv_feat + kv_taps[tap_index] * kv_all[:, offset : offset + kv_span]
    gated_kv = kv_feat[:, :, :chan_local] * kv_feat[:, :, chan_local:]

    def add_tap(tap_index, running):
        shifted = lax.dynamic_slice_in_dim(gated_kv, KL - 1 - tap_index, row_count, 1)
        return running + long_taps[tap_index] * shifted

    filtered = lax.fori_loop(0, KL, add_tap, jnp.zeros_like(q_feat))
    y_out = (q_feat * filtered).astype(jnp.bfloat16)
    partial_terms = jnp.einsum("snc,cd->snd", y_out, w_down[0], preferred_element_type=jnp.float32)
    mixed = lax.psum_scatter(
        partial_terms.astype(jnp.bfloat16), "tensor", scatter_dimension=2, tiled=True
    ).astype(jnp.float32)
    return (stream.astype(jnp.float32) + mixed).astype(jnp.bfloat16)


def local(token_ids, embed_table, in_proj, feat_taps, se_taps, mr_taps, out_proj, norm_gain):
    section = lax.axis_index("pipe")
    shard_pos = lax.axis_index("seq")
    lead_segment = section == 0
    padded_se = jnp.concatenate(
        [se_taps, jnp.zeros((KL - KS, se_taps.shape[1]), jnp.float32)], axis=0
    )
    long_taps = jnp.where(lead_segment, padded_se, mr_taps)
    w_flat = in_proj[0].reshape(in_proj.shape[1], -1)
    vocab_ids = jnp.arange(VOCAB, dtype=jnp.int32)
    one_hot = (token_ids[:, :, None] == vocab_ids[None, None, :]).astype(jnp.bfloat16)
    embedded = jnp.einsum(
        "snv,vd->snd", one_hot, embed_table, preferred_element_type=jnp.float32
    ).astype(jnp.bfloat16)
    current = jnp.where(lead_segment, embedded, jnp.zeros_like(embedded))
    outputs = []
    for step_index in range(SEGMENTS):
        projected = project(current, w_flat, norm_gain)
        kv_recv, q_recv = send_tails(projected)
        kv_earlier = jnp.concatenate([jnp.zeros_like(kv_recv[:1]), kv_recv[:-1]], axis=0)
        q_earlier = jnp.concatenate([jnp.zeros_like(q_recv[:1]), q_recv[:-1]], axis=0)
        kv_prev = jnp.where(shard_pos == 0, kv_earlier, kv_recv)
        q_prev = jnp.where(shard_pos == 0, q_earlier, q_recv)
        result = mixing(current, projected, kv_prev, q_prev, feat_taps, long_taps, out_proj)
        outputs.append(result)
        if step_index + 1 < SEGMENTS:
            current = hand_over(result)
    final_out = lax.dynamic_index_in_dim(jnp.stack(outputs, axis=0), section, 0, keepdims=True)
    return final_out


def solution(mesh):
    return jax.shard_map(
        local,
        mesh=mesh,
        in_specs=(
            P(None, "seq"),
            P(None, "tensor"),
            P("pipe", None, None, "tensor"),
            P("pipe", None, None, "tensor"),
            P(None, "tensor"),
            P(None, "tensor"),
            P("pipe", "tensor", None),
            P("pipe", "tensor"),
        ),
        out_specs=P("pipe", None, "seq", "tensor"),
        check_vma=False,
    )
```

profile of v0, /device:TPU:4, one launch (start us, length us, event | category | flops | bytes accessed | tf_op | source)
XLA Modules:
  0.0 731.5 jit_solution(4473578818724126440)
XLA Ops:
  6.5 2.1 fusion.22
  8.8 8.7 %copy.9 = bf16[1,8192,3,128]{1,3,2,0:T(8,128)(2,1)} copy(bf16[1,8192,3,128]{3,1,2,0:T(8,128)(2,1)} %param.14) | data formatting | bytes 12582912 | tf_op args[2]
  17.5 46.2 %all_gather.11 = bf16[1,8192]{1,0:T(2,128)(2,1)S(1)} all-gather(bf16[1,256]{1,0:T(2,128)(2,1)S(1)} %copy-done.9), channel_id=1, replica_groups=mesh['pipe'=2,'seq'=4,'tensor'=32] {'tensor'}, dimensions={1}, use_global_device_ids=true | all-gather | bytes 16896 | tf_op jit(solution)/shard_map/all_gather | solution.py:32
  63.8 41.7 %all-gather.3.cloned.1.call-done = bf16[2,192,8192]{2,1,0:T(8,128)(2,1)} async-done(((bf16[2,192,256]{2,1,0:T(8,128)(2,1)}), bf16[2,192,8192]{2,1,0:T(8,128)(2,1)}) %all-gather.3.cloned.1.call-update) | async-done | bytes 6291472 | tf_op jit(solution)/shard_map/all_gather | solution.py:31
  105.5 4.3 fusion
  109.8 0.3 copy-done.1
  110.1 5.8 fusion.16
  115.9 1.2 collective-permute-start
  117.3 0.7 collective-permute-start.1
  117.9 1.7 collective-permute-done
  119.6 2.8 collective-permute-done.1
  122.7 16.4 %while.32 = (s32[]{:T(128)}, f32[2,192,128]{2,1,0:T(8,128)S(1)}, f32[128,128]{1,0:T(8,128)S(1)}, f32[2,319,128]{2,1,0:T(8,128)S(1)}, s32[]{:T(128)}, /*index=5*/s32[]{:T(128)}, s32[]{:T(128)}, s32[]{:T(128)}) while((s32[]{:T(128)}, f32[2,192,128]{2,1,0:T(8,128)S(1)}, f32[128,128]{1,0:T(8,128)S(1)}, f32[2,319,128]{2,1,0:T(8,128)S(1)}, ...), condition=%wide.region_2.3_spmd.clone, body=%wide.region_1.2_spmd.clone.sunk | while | flops 147463 | bytes 591509 | solution.py:73
  139.2 4.4 convolution_convert_fusion.1
  143.7 223.0 %reduce-scatter.3.cloned.1.call-done = bf16[2,192,256]{2,1,0:T(8,128)(2,1)} async-done(((bf16[2,192,8192]{2,1,0:T(8,128)(2,1)}), bf16[2,192,256]{2,1,0:T(8,128)(2,1)}) %reduce-scatter.3.cloned.1.call-update) | async-done | bytes 196624 | tf_op jit(solution)/shard_map/reduce_scatter | solution.py:76
  366.7 1.0 add_convert_fusion.1
  367.7 1.3 collective-permute-start.2
  369.0 1.0 collective-permute-done.2
  370.0 0.7 copy-done.4
  370.7 0.2 reduce-scatter.5.cloned.1.call-start
  370.9 90.8 %all-gather.5.cloned.1.call-done = bf16[2,192,8192]{2,1,0:T(8,128)(2,1)} async-done(((bf16[2,192,256]{2,1,0:T(8,128)(2,1)}), bf16[2,192,8192]{2,1,0:T(8,128)(2,1)}) %all-gather.5.cloned.1.call-update) | async-done | bytes 6291472 | tf_op jit(solution)/shard_map/all_gather | solution.py:31
  461.8 4.3 fusion.3
  466.0 0.3 copy-done.2
  466.4 6.2 fusion.19
  472.6 1.3 collective-permute-start.3
  474.0 0.6 collective-permute-start.4
  474.6 1.7 collective-permute-done.3
  476.3 2.8 collective-permute-done.4
  479.5 16.4 %while.33 = (s32[]{:T(128)}, f32[2,192,128]{2,1,0:T(8,128)S(1)}, f32[128,128]{1,0:T(8,128)S(1)}, f32[2,319,128]{2,1,0:T(8,128)S(1)}, s32[]{:T(128)}, /*index=5*/s32[]{:T(128)}, s32[]{:T(128)}, s32[]{:T(128)}) while((s32[]{:T(128)}, f32[2,192,128]{2,1,0:T(8,128)S(1)}, f32[128,128]{1,0:T(8,128)S(1)}, f32[2,319,128]{2,1,0:T(8,128)S(1)}, ...), condition=%wide.region_6.7_spmd.clone, body=%wide.region_5.6_spmd.clone.sunk | while | flops 147463 | bytes 591509 | solution.py:73
  495.9 4.5 convolution_convert_fusion
  500.4 222.8 %reduce-scatter.5.cloned.1.call-done = bf16[2,192,256]{2,1,0:T(8,128)(2,1)} async-done(((bf16[2,192,8192]{2,1,0:T(8,128)(2,1)}), bf16[2,192,256]{2,1,0:T(8,128)(2,1)}) %reduce-scatter.5.cloned.1.call-update) | async-done | bytes 196624 | tf_op jit(solution)/shard_map/reduce_scatter | solution.py:76
  723.2 1.0 fusion.29
  724.2 0.8 fusion.30
  (568 shorter events, 24.4 us)
Async XLA Ops:
  6.5 132.6 %copy-start = (bf16[1,128,8192]{2,1,0:T(8,128)(2,1)S(1)}, bf16[1,128,8192]{2,1,0:T(8,128)(2,1)}, u32[]{:S(2)}) copy-start(bf16[1,128,8192]{2,1,0:T(8,128)(2,1)} %param.18) | copy-start | bytes 6291460
  6.5 99.0 %all-gather.3.cloned.1.call-start = ((), (), s32[]{:S(2)}) async-start(), calls=%async_computation.2 | async-start | bytes 6488064 | tf_op jit(solution)/shard_map/all_gather | solution.py:31
  8.7 8.8 %copy-start.9 = (bf16[1,256]{1,0:T(2,128)(2,1)S(1)}, bf16[1,256]{1,0:T(2,128)(2,1)}, u32[]{:S(2)}) copy-start(bf16[1,256]{1,0:T(2,128)(2,1)} %param.19) | copy-start | bytes 1540
  8.7 55.1 %copy-start.7 = (f32[1,3,3,128]{3,0,2,1:T(1,128)S(1)}, f32[1,3,3,128]{3,0,2,1:T(1,128)}, u32[]{:S(2)}) copy-start(f32[1,3,3,128]{3,0,2,1:T(1,128)} %param.15) | copy-start | bytes 13828
  8.7 55.1 %copy-start.6 = (f32[128,128]{1,0:T(8,128)S(1)}, f32[128,128]{1,0:T(8,128)}, u32[]{:S(2)}) copy-start(f32[128,128]{1,0:T(8,128)} %param.17) | copy-start | bytes 196612
  8.7 55.1 %copy-start.8 = (f32[7,128]{1,0:T(8,128)S(1)}, f32[7,128]{1,0:T(8,128)}, u32[]{:S(2)}) copy-start(f32[7,128]{1,0:T(8,128)} %param.16) | copy-start | bytes 10756
  8.7 358.0 %reduce-scatter.3.cloned.1.call-start = ((), (), s32[]{:S(2)}) async-start(), calls=%async_computation.3 | async-start | bytes 6488064 | tf_op jit(solution)/shard_map/reduce_scatter | solution.py:76
  105.5 4.6 copy-start.1
  115.9 3.6 collective-permute-start
  117.3 5.1 collective-permute-start.1
  139.2 227.5 %copy-start.3 = (bf16[2,192,256]{2,1,0:T(8,128)(2,1)S(1)}, bf16[2,192,256]{2,1,0:T(8,128)(2,1)}, u32[]{:S(2)}) copy-start(bf16[2,192,256]{2,1,0:T(8,128)(2,1)} %fusion.22) | copy-start | bytes 589828
  143.6 318.2 %all-gather.5.cloned.1.call-start = ((), (), s32[]{:S(2)}) async-start(), calls=%async_computation.4 | async-start | bytes 6488064 | tf_op jit(solution)/shard_map/all_gather | solution.py:31
  367.7 2.4 collective-permute-start.2
  370.0 0.7 copy-start.4
  370.7 352.5 %reduce-scatter.5.cloned.1.call-start = ((), (), s32[]{:S(2)}) async-start(), calls=%async_computation.5 | async-start | bytes 6488064 | tf_op jit(solution)/shard_map/reduce_scatter | solution.py:76
  461.8 4.6 copy-start.2
  472.6 3.6 collective-permute-start.3
  474.0 5.1 collective-permute-start.4
  495.9 227.3 %copy-start.5 = (bf16[2,192,256]{2,1,0:T(8,128)(2,1)S(1)}, bf16[2,192,256]{2,1,0:T(8,128)(2,1)}, u32[]{:S(2)}) copy-start(bf16[2,192,256]{2,1,0:T(8,128)(2,1)} %copy-done.4) | copy-start | bytes 589828
Sparse Core Ops, SparseCore 0:
  9.8 95.6 all-gather.2
  143.7 222.8 reduce-scatter.2
  370.8 90.9 all-gather.4
  500.5 222.6 reduce-scatter.4
where the time goes:
time: 732 us; the launch traced here: 731 us
  waiting for transfers between devices  588 us (80%)
  blocking collectives  46.2 us (6%)
  other arithmetic  32.8 us (4%)
  matrix products  23.1 us (3%)
  between operations  13.4 us (2%)
  local copies, waits for them, and re-layouts  12.7 us (2%)
  loops' own time  9.56 us (1%)
    reduce_scatter x2, waiting for transfers between devices, mixing(): lax.psum_scatter(partial_terms.astype(jnp.bfloat16), 'tensor', scatter_di...  446 us
    all_gather x2, waiting for transfers between devices, project(): lax.all_gather(stream, 'tensor', axis=2, tiled=True)  132 us
    all_gather x1, blocking collectives, project(): lax.all_gather(gain_cols, 'tensor', axis=1, tiled=True)  46.2 us
    add x256, other arithmetic, add_tap(): return running + long_taps[tap_index] * shifted  20.9 us
  transfers between devices with their start and end apart: 9, of which 9 were waited for; matrix products, arithmetic and copies ran while one was open for 1% of the time, Pallas kernels for 0%

commit v1 on v0

v1 whole, which is shorter than its diff:
```python
import jax
import jax.numpy as jnp
from jax import lax
from jax.sharding import PartitionSpec as P

VOCAB = 512
KL = 128
KS = 7
KF = 3
HALO = KL + KF - 2


epsilon = 1e-06


def swapped(value):
    return lax.ppermute(value, "pipe", [(0, 1), (1, 0)])


def of_section(core, own, other, section):
    return jnp.where(core == section, own, other)


def relaid_out_proj(w_down):
    n_t = lax.axis_size("tensor")
    chan_local, width = w_down.shape
    blocks = w_down.reshape(chan_local, n_t, width // n_t)
    moved = lax.all_to_all(blocks, "tensor", 1, 0, tiled=True)
    return moved.reshape(n_t * chan_local, width // n_t)


def section_step(x_in, w_in, feat, long_taps, w_out, gain):
    rows = x_in.shape[0]
    chan_local = w_in.shape[1] // 3
    aug = jnp.concatenate([x_in, gain.reshape(1, -1).astype(x_in.dtype)], axis=0)
    full = lax.all_gather(aug, "tensor", axis=1, tiled=True)
    values = full[:rows].astype(jnp.float32)
    gain_all = full[rows].astype(jnp.float32)
    inv_rms = lax.rsqrt(jnp.mean(values * values, axis=1, keepdims=True) + epsilon)
    normed = (values * inv_rms * gain_all[None, :]).astype(jnp.bfloat16)
    projected = jnp.dot(normed, w_in, preferred_element_type=jnp.float32).astype(jnp.bfloat16)

    blocks = lax.axis_size("pipe") * lax.axis_size("seq")
    kv_tail = projected[rows - HALO :, chan_local:]
    q_tail = projected[rows - (KF - 1) :, :chan_local]
    kv_prev, q_prev = lax.ppermute(
        (kv_tail, q_tail), ("pipe", "seq"), [(b, b + 1) for b in range(blocks - 1)]
    )

    q_all = jnp.concatenate([q_prev, projected[:, :chan_local]], axis=0).astype(jnp.float32)
    kv_all = jnp.concatenate([kv_prev, projected[:, chan_local:]], axis=0).astype(jnp.float32)
    q_taps = feat[:, 0, :]
    kv_taps = feat[:, 1:, :].reshape(KF, 2 * chan_local)
    kv_span = KL - 1 + rows
    q_feat = jnp.zeros((rows, chan_local), jnp.float32)
    kv_feat = jnp.zeros((kv_span, 2 * chan_local), jnp.float32)
    for tap_index in range(KF):
        offset = KF - 1 - tap_index
        q_feat = q_feat + q_taps[tap_index] * q_all[offset : offset + rows]
        kv_feat = kv_feat + kv_taps[tap_index] * kv_all[offset : offset + kv_span]
    gated_kv = kv_feat[:, :chan_local] * kv_feat[:, chan_local:]

    def add_tap(tap_index, running):
        shifted = lax.dynamic_slice_in_dim(gated_kv, KL - 1 - tap_index, rows, 0)
        return running + long_taps[tap_index] * shifted

    filtered = lax.fori_loop(0, KL, add_tap, jnp.zeros_like(q_feat))
    y_out = (q_feat * filtered).astype(jnp.bfloat16)
    y_full = lax.all_gather(y_out, "tensor", axis=1, tiled=True)
    mixed = jnp.dot(y_full, w_out, preferred_element_type=jnp.float32)
    return (x_in.astype(jnp.float32) + mixed).astype(jnp.bfloat16)


def local(token_ids, embed_table, in_proj, feat_taps, se_taps, mr_taps, out_proj, norm_gain):
    core = lax.axis_index("pipe")

    w_own = in_proj[0].reshape(in_proj.shape[1], -1)
    feat_own = feat_taps[0]
    gain_own = norm_gain[0]
    wt_own = relaid_out_proj(out_proj[0])
    w_other, feat_other, gain_other, wt_other = swapped((w_own, feat_own, gain_own, wt_own))

    padded_se = jnp.concatenate(
        [se_taps, jnp.zeros((KL - KS, se_taps.shape[1]), jnp.float32)], axis=0
    )
    filters = (padded_se, mr_taps)

    ids = lax.dynamic_index_in_dim(token_ids, core, 0, keepdims=False)
    vocab_ids = jnp.arange(VOCAB, dtype=jnp.int32)
    one_hot = (ids[:, None] == vocab_ids[None, :]).astype(jnp.bfloat16)
    current = jnp.dot(one_hot, embed_table, preferred_element_type=jnp.float32).astype(
        jnp.bfloat16
    )

    results = []
    for section in range(2):
        current = section_step(
            current,
            of_section(core, w_own, w_other, section),
            of_section(core, feat_own, feat_other, section),
            filters[section],
            of_section(core, wt_own, wt_other, section),
            of_section(core, gain_own, gain_other, section),
        )
        results.append(current)

    first_mine, second_mine = results
    second_slice_of_first = lax.ppermute(first_mine, "pipe", [(1, 0)])
    first_slice_of_second = lax.ppermute(second_mine, "pipe", [(0, 1)])
    lead = core == 0
    slice_zero = jnp.where(lead, first_mine, first_slice_of_second)
    slice_one = jnp.where(lead, second_slice_of_first, second_mine)
    return jnp.stack([slice_zero, slice_one], axis=0)[None]


def solution(mesh):
    return jax.shard_map(
        local,
        mesh=mesh,
        in_specs=(
            P(None, "seq"),
            P(None, "tensor"),
            P("pipe", None, None, "tensor"),
            P("pipe", None, None, "tensor"),
            P(None, "tensor"),
            P(None, "tensor"),
            P("pipe", "tensor", None),
            P("pipe", "tensor"),
        ),
        out_specs=P("pipe", None, "seq", "tensor"),
        check_vma=False,
    )
```

time: 732 us -> 502 us (0.69)
  waiting for transfers between devices: 588 us -> 307 us
  local copies, waits for them, and re-layouts: 12.7 us -> 105 us
  blocking collectives: 46.2 us -> 0 us
  starting transfers between devices: 5.37 us -> 25 us
  other arithmetic: 32.8 us -> 19.8 us
    reduce_scatter x2 -> x0, waiting for transfers between devices: 446 us -> none  [mixing(): lax.psum_scatter(partial_terms.astype(jnp.bfloat16), 'tensor', scatter_di...]
    all_gather x2 -> x4, waiting for transfers between devices: 132 us -> 293 us  [the longest x2 157 us: section_step(): full = lax.all_gather(aug, 'tensor', axis=1, tiled=True)]
    mul x256, local copies, waits for them, and re-layouts: 2.43 us -> 90.3 us  [add_tap(): return running + long_taps[tap_index] * shifted]
    all_gather x1 -> x0, blocking collectives: 46.2 us -> none  [project(): lax.all_gather(gain_cols, 'tensor', axis=1, tiled=True)]
    add x256, other arithmetic: 20.9 us -> 8.22 us  [add_tap(): return running + long_taps[tap_index] * shifted]
    all_to_all x0 -> x1, starting transfers between devices: none -> 11.5 us  [relaid_out_proj(): moved = lax.all_to_all(blocks, 'tensor', 1, 0, tiled=True)]
    ppermute x5 -> x10, starting transfers between devices: 5.07 us -> 13.4 us  [the longest x4 10.2 us: section_step(): lax.ppermute((kv_tail, q_tail), ('pipe', 'seq'), [(b, b + 1) for b in ran...]
  transfers between devices with their start and end apart: 9 -> 15, of which waited for: 9 -> 11; matrix products, arithmetic and copies ran while one was open for 1% -> 7% of each run, Pallas kernels for 0% -> 0%
where the time goes in v1:
time: 502 us; the launch traced here: 496 us
  waiting for transfers between devices  307 us (61%)
  local copies, waits for them, and re-layouts  105 us (21%)
  starting transfers between devices  25 us (5%)
  other arithmetic  19.8 us (4%)
  matrix products  17.5 us (3%)
  between operations  13.5 us (3%)
  loops' own time  8.15 us (2%)
    all_gather x2, waiting for transfers between devices, section_step(): full = lax.all_gather(aug, 'tensor', axis=1, tiled=True)  157 us
    all_gather x2, waiting for transfers between devices, section_step(): y_full = lax.all_gather(y_out, 'tensor', axis=1, tiled=True)  136 us
    mul x256, local copies, waits for them, and re-layouts, add_tap(): return running + long_taps[tap_index] * shifted  90.3 us
    dot_general x2, matrix products, section_step(): jnp.dot(normed, w_in, preferred_element_type=jnp.float32)  12 us
    all_to_all x1, starting transfers between devices, relaid_out_proj(): moved = lax.all_to_all(blocks, 'tensor', 1, 0, tiled=True)  11.5 us
    unnamed x15, local copies, waits for them, and re-layouts  11.3 us
    ppermute x4, starting transfers between devices, section_step(): lax.ppermute((kv_tail, q_tail), ('pipe', 'seq'), [(b, b + 1) for b in ran...  10.2 us
  transfers between devices with their start and end apart: 15, of which 11 were waited for; matrix products, arithmetic and copies ran while one was open for 7% of the time, Pallas kernels for 0%

profile of v1, /device:TPU:4, one launch (start us, length us, event | category | flops | bytes accessed | tf_op | source)
XLA Modules:
  0.0 496.3 jit_solution(15193292453883227668)
XLA Ops:
  6.5 0.7 reduce
  9.2 8.9 %copy.10 = bf16[1,8192,3,128]{1,3,2,0:T(8,128)(2,1)} copy(bf16[1,8192,3,128]{3,1,2,0:T(8,128)(2,1)} %param.14) | data formatting | bytes 12582912 | tf_op args[2]
  18.6 2.4 copy.11
  21.1 11.5 %all-to-all-start = ((bf16[128,32,256]{0,2,1:T(8,128)(2,1)}), bf16[128,32,256]{0,2,1:T(8,128)(2,1)S(1)}, u32[]{:S(2)}, u32[]{:S(2)}) async-start(bf16[128,32,256]{0,2,1:T(8,128)(2,1)} %bitcast.58), calls=%async_computation | async-start | bytes 4194304 | tf_op jit(solution)/shard_map/all_to_all | solution.py:28
  32.7 78.8 %all-gather.5.cloned.1.call-done = bf16[193,8192]{1,0:T(8,128)(2,1)} async-done(((bf16[193,256]{1,0:T(8,128)(2,1)}), bf16[193,8192]{1,0:T(8,128)(2,1)}) %all-gather.5.cloned.1.call-update) | async-done | bytes 3162128 | tf_op jit(solution)/shard_map/all_gather | solution.py:36
  111.5 2.6 fusion
  114.1 0.9 slice_convert_fusion.1
  115.0 6.0 %fusion.26 = bf16[192,384]{1,0:T(8,128)(2,1)S(1)} fusion(bf16[8192,384]{0,1:T(8,128)(2,1)} %bitcast.60, bf16[8192,384]{0,1:T(8,128)(2,1)} %collective-permute-done.2, pred[]{:T(512)S(6)} %eq.12, f32[8192]{0:T(1024)S(1)} %bitcast.65, f32[192]{0:T(256)S(1)} %add_rsqrt_fusion.1, bf16[193,8192]{1,0:T(8,128)(2,1)} %all-gather.5.cloned.1.call-done), kind=kOutput, calls=%fused_computation.32 | convolution fusion | flops 1217470464 | bytes 15909633 | tf_op jit(solution)/shard_map/dot_general | solution.py:41
  121.0 3.1 collective-permute-start.3
  124.2 1.9 collective-permute-start.4
  126.5 3.9 collective-permute-done.4
  130.6 10.6 %while.32 = (s32[]{:T(128)}, f32[192,128]{1,0:T(8,128)S(1)}, f32[128,128]{1,0:T(8,128)S(1)}, f32[319,128]{1,0:T(8,128)S(1)}, s32[]{:T(128)}, /*index=5*/s32[]{:T(128)}, s32[]{:T(128)}, s32[]{:T(128)}) while((s32[]{:T(128)}, f32[192,128]{1,0:T(8,128)S(1)}, f32[128,128]{1,0:T(8,128)S(1)}, f32[319,128]{1,0:T(8,128)S(1)}, s32[]{:T(128)}, ...), condition=%wide.region_2.3_spmd.clone, body=%wide.region_1.2_spmd.clone.sunk | while | flops 73735 | bytes 296597 | solution.py:67
  142.0 2.9 copy.12
  144.9 4.4 collective-permute-done.5
  149.3 63.7 %all-gather.7.cloned.1.call-done = bf16[192,4096]{1,0:T(8,128)(2,1)} async-done(((bf16[192,128]{1,0:T(8,128)(2,1)}), bf16[192,4096]{1,0:T(8,128)(2,1)}) %all-gather.7.cloned.1.call-update) | async-done | bytes 1572880 | tf_op jit(solution)/shard_map/all_gather | solution.py:69
  213.0 2.7 fusion.39
  216.4 78.4 %all-gather.9.cloned.1.call-done = bf16[193,8192]{1,0:T(8,128)(2,1)} async-done(((bf16[193,256]{1,0:T(8,128)(2,1)}), bf16[193,8192]{1,0:T(8,128)(2,1)}) %all-gather.9.cloned.1.call-update) | async-done | bytes 3162128 | tf_op jit(solution)/shard_map/all_gather | solution.py:36
  294.8 2.6 fusion.3
  297.4 0.9 slice_convert_fusion
  298.3 6.0 %fusion.31 = bf16[192,384]{1,0:T(8,128)(2,1)S(1)} fusion(bf16[8192,384]{0,1:T(8,128)(2,1)} %bitcast.61, bf16[8192,384]{0,1:T(8,128)(2,1)} %collective-permute-done.2, pred[]{:T(512)S(6)} %eq.33, f32[8192]{0:T(1024)S(1)} %bitcast.66, f32[192]{0:T(256)S(1)} %add_rsqrt_fusion, bf16[193,8192]{1,0:T(8,128)(2,1)} %all-gather.9.cloned.1.call-done), kind=kOutput, calls=%fused_computation.33 | convolution fusion | flops 1217470464 | bytes 15909633 | tf_op jit(solution)/shard_map/dot_general | solution.py:41
  304.4 3.2 collective-permute-start.6
  307.7 1.9 collective-permute-start.7
  309.9 3.9 collective-permute-done.7
  314.0 96.0 %while.33 = (s32[]{:T(128)}, f32[192,128]{1,0:T(8,128)S(1)}, f32[128,128]{1,0:T(8,128)}, f32[319,128]{1,0:T(8,128)S(1)}, s32[]{:T(128)}, /*index=5*/s32[]{:T(128)}, s32[]{:T(128)}, s32[]{:T(128)}) while((s32[]{:T(128)}, f32[192,128]{1,0:T(8,128)S(1)}, f32[128,128]{1,0:T(8,128)}, f32[319,128]{1,0:T(8,128)S(1)}, s32[]{:T(128)}, ...), condition=%wide.region_5.6_spmd.clone, body=%wide.region_4.5_spmd.clone.sunk | while | flops 73735 | bytes 296597 | solution.py:67
  314.0 0.7 dynamic-slice_bitcast_fusion.5
  314.8 0.7 dynamic-slice_bitcast_fusion.5
  410.7 1.3 collective-permute-start.9
  412.0 72.1 %all-gather.11.cloned.1.call-done = bf16[192,4096]{1,0:T(8,128)(2,1)} async-done(((bf16[192,128]{1,0:T(8,128)(2,1)}), bf16[192,4096]{1,0:T(8,128)(2,1)}) %all-gather.11.cloned.1.call-update) | async-done | bytes 1572880 | tf_op jit(solution)/shard_map/all_gather | solution.py:69
  484.1 2.7 fusion.20
  486.8 1.3 collective-permute-start.8
  488.1 0.9 collective-permute-done.8
  489.1 0.7 maximum_bitcast_fusion
  (579 shorter events, 102.9 us)
Async XLA Ops:
  6.5 1.5 copy-start
  6.5 104.9 %all-gather.5.cloned.1.call-start = ((), (), s32[]{:S(2)}) async-start(), calls=%async_computation.1 | async-start | bytes 3379200 | tf_op jit(solution)/shard_map/all_gather | solution.py:36
  7.3 1.2 collective-permute-start.1
  9.2 9.3 %copy-start.3 = (f32[1,3,3,128]{3,0,2,1:T(1,128)S(1)}, f32[1,3,3,128]{3,0,2,1:T(1,128)}, u32[]{:S(2)}) copy-start(f32[1,3,3,128]{3,0,2,1:T(1,128)} %param.15) | copy-start | bytes 13828
  9.2 9.4 %copy-start.1 = (bf16[1,128,8192]{2,1,0:T(8,128)(2,1)S(1)}, bf16[1,128,8192]{2,1,0:T(8,128)(2,1)}, u32[]{:S(2)}) copy-start(bf16[1,128,8192]{2,1,0:T(8,128)(2,1)} %param.18) | copy-start | bytes 6291460
  18.1 97.0 %collective-permute-start.2 = (bf16[8192,384]{0,1:T(8,128)(2,1)}, bf16[8192,384]{0,1:T(8,128)(2,1)}, u32[]{:S(2)}, u32[]{:S(2)}) collective-permute-start(bf16[8192,384]{0,1:T(8,128)(2,1)} %bitcast.59), channel_id=1, source_target_pairs={{0,128},{128,0},{1,129},{129,1},{2,130},{130,2},{3,131},{131,3},{4... | collective-permute-start | bytes 18874376 | tf_op jit(solution)/shard_map/ppermute | solution.py:17
  18.4 14.2 %copy-start.4 = (f32[7,128]{1,0:T(8,128)S(1)}, f32[7,128]{1,0:T(8,128)}, u32[]{:S(2)}) copy-start(f32[7,128]{1,0:T(8,128)} %param.16) | copy-start | bytes 10756
  18.4 14.2 %collective-permute-start = (f32[3,3,128]{2,1,0:T(4,128)S(1)}, f32[3,3,128]{2,1,0:T(4,128)S(1)}, u32[]{:S(2)}, u32[]{:S(2)}) collective-permute-start(f32[3,3,128]{2,1,0:T(4,128)S(1)} %bitcast.67), channel_id=1, source_target_pairs={{0,128},{128,0},{1,129},{129,1},{2,130},{130,2},{3,131},{131,3},{4... | collective-permute-start | bytes 13832 | tf_op jit(solution)/shard_map/ppermute | solution.py:17
  21.1 120.9 %all-to-all-start = ((bf16[128,32,256]{0,2,1:T(8,128)(2,1)}), bf16[128,32,256]{0,2,1:T(8,128)(2,1)S(1)}, u32[]{:S(2)}, u32[]{:S(2)}) async-start(bf16[128,32,256]{0,2,1:T(8,128)(2,1)} %bitcast.58), calls=%async_computation | async-start | bytes 4194304 | tf_op jit(solution)/shard_map/all_to_all | solution.py:28
  32.6 180.4 %all-gather.7.cloned.1.call-start = ((), (), s32[]{:S(2)}) async-start(), calls=%async_computation.2 | async-start | bytes 1622016 | tf_op jit(solution)/shard_map/all_gather | solution.py:69
  121.0 5.4 %collective-permute-start.3 = (bf16[2,128]{1,0:T(2,128)(2,1)S(1)}, bf16[2,128]{1,0:T(2,128)(2,1)S(1)}, u32[]{:S(2)}, u32[]{:S(2)}) collective-permute-start(bf16[2,128]{1,0:T(2,128)(2,1)S(1)} %slice.191), channel_id=1, source_target_pairs={{0,32},{32,64},{64,96},{96,128},{128,160},{160,192},{192,224},{1,3... | collective-permute-start | bytes 1544 | tf_op jit(solution)/shard_map/ppermute | solution.py:46
  124.2 6.2 %collective-permute-start.4 = (bf16[129,256]{1,0:T(8,128)(2,1)S(1)}, bf16[129,256]{1,0:T(8,128)(2,1)S(1)}, u32[]{:S(2)}, u32[]{:S(2)}) collective-permute-start(bf16[129,256]{1,0:T(8,128)(2,1)S(1)} %slice.199), channel_id=1, source_target_pairs={{0,32},{32,64},{64,96},{96,128},{128,160},{160,192},{192,224},{1,3... | collective-permute-start | bytes 198152 | tf_op jit(solution)/shard_map/ppermute | solution.py:46
  141.9 152.9 %all-gather.9.cloned.1.call-start = ((), (), s32[]{:S(2)}) async-start(), calls=%async_computation.3 | async-start | bytes 3379200 | tf_op jit(solution)/shard_map/all_gather | solution.py:36
  144.9 4.4 collective-permute-start.5
  149.3 66.4 %copy-start.5 = (bf16[4096,256]{1,0:T(8,128)(2,1)}, bf16[4096,256]{1,0:T(8,128)(2,1)S(1)}, u32[]{:S(2)}) copy-start(bf16[4096,256]{1,0:T(8,128)(2,1)S(1)} %collective-permute-done.5) | copy-start | bytes 6291460
  216.3 267.8 %all-gather.11.cloned.1.call-start = ((), (), s32[]{:S(2)}) async-start(), calls=%async_computation.4 | async-start | bytes 1622016 | tf_op jit(solution)/shard_map/all_gather | solution.py:69
  304.3 179.8 %copy-start.2 = (bf16[32,128,1,256]{3,1,0,2:T(8,128)(2,1)S(1)}, bf16[32,128,1,256]{3,1,0,2:T(8,128)(2,1)}, u32[]{:S(2)}) copy-start(bf16[32,128,1,256]{3,1,0,2:T(8,128)(2,1)} %copy.12) | copy-start | bytes 6291460
  304.4 5.6 %collective-permute-start.6 = (bf16[2,128]{1,0:T(2,128)(2,1)S(1)}, bf16[2,128]{1,0:T(2,128)(2,1)S(1)}, u32[]{:S(2)}, u32[]{:S(2)}) collective-permute-start(bf16[2,128]{1,0:T(2,128)(2,1)S(1)} %slice.211), channel_id=1, source_target_pairs={{0,32},{32,64},{64,96},{96,128},{128,160},{160,192},{192,224},{1,3... | collective-permute-start | bytes 1544 | tf_op jit(solution)/shard_map/ppermute | solution.py:46
  307.7 6.2 %collective-permute-start.7 = (bf16[129,256]{1,0:T(8,128)(2,1)S(1)}, bf16[129,256]{1,0:T(8,128)(2,1)S(1)}, u32[]{:S(2)}, u32[]{:S(2)}) collective-permute-start(bf16[129,256]{1,0:T(8,128)(2,1)S(1)} %slice.219), channel_id=1, source_target_pairs={{0,32},{32,64},{64,96},{96,128},{128,160},{160,192},{192,224},{1,3... | collective-permute-start | bytes 198152 | tf_op jit(solution)/shard_map/ppermute | solution.py:46
  410.7 76.0 %collective-permute-start.9 = (bf16[192,256]{1,0:T(8,128)(2,1)S(1)}, bf16[192,256]{1,0:T(8,128)(2,1)S(1)}, u32[]{:S(2)}, u32[]{:S(2)}) collective-permute-start(bf16[192,256]{1,0:T(8,128)(2,1)S(1)} %fusion.39), channel_id=1, source_target_pairs={{128,0},{129,1},{130,2},{131,3},{132,4},{133,5},{134,6},{135,7},{1... | collective-permute-start | bytes 294920 | tf_op jit(solution)/shard_map/ppermute | solution.py:108
  486.8 2.2 collective-permute-start.8
Sparse Core Ops, SparseCore 0:
  9.8 101.6 all-gather.4
  142.1 70.8 all-gather.6
  216.4 78.3 all-gather.8
  410.8 73.2 all-gather.10
